TPU v7x, 256 devices: a whole 4x4x8 slice. The times are simulated.
256 devices in a mesh: row: 16 (over z, core), col: 16 (over y, x).
Axes of the slice: x: 4, y: 4, z: 8, core: 2. Of those that a mesh axis runs over, the one named last changes fastest.
Arguments:
- matrix: bfloat16 [4096, 262144], P('row', 'col'), may hold values from -60 to 60
- test_matrix: bfloat16 [262144, 512], P(('col', 'row')), may hold values from -0.0390625 to 0.0390625
Outputs:
- orthonormal: float32 [4096, 512], P(('row', 'col'))
- triangular: float32 [512, 512], replicated
All inputs are finite; a program needn't handle non-finite values.
Results may differ from a plain program's by a relative error of at most 0.0003.
Values may be sent and summed in bfloat16 or wider, within the bound.
No kernel may reach another device: no remote copies, remote signals or barrier semaphores. Data moves between devices by JAX's collectives and lax.ppermute only.
A program may use at most 128 MiB of HBM per device.

v0:
```python
import jax
import jax.numpy as jnp
from jax import lax
from jax.sharding import PartitionSpec as P


def probe_product(matrix, test_matrix):
    return jnp.dot(
        matrix,
        lax.all_gather(test_matrix, "row", axis=0, tiled=True),
        preferred_element_type=jnp.float32,
    )


def gram_term(own_rows):
    return jnp.dot(own_rows.T, own_rows, precision=lax.Precision.HIGHEST)


def shards(matrix, test_matrix):
    share_rows = matrix.shape[0] // lax.axis_size("col")
    total_rows = matrix.shape[0] * lax.axis_size("row")
    partial_value = probe_product(matrix, test_matrix)
    sketch = lax.psum(partial_value, "col")
    gram = lax.psum(gram_term(sketch), "row")
    own_rows = lax.dynamic_slice_in_dim(sketch, lax.axis_index("col") * share_rows, share_rows, 0)
    gram = gram / jnp.float32(total_rows)
    lower_factor = jnp.linalg.cholesky(gram)
    orthonormal = lax.linalg.triangular_solve(
        lower_factor, own_rows, left_side=False, lower=True, transpose_a=True
    )
    return (orthonormal, lower_factor.T)


def solution(mesh):
    in_specs = (P("row", "col"), P(("col", "row"), None))
    out_specs = (P(("row", "col"), None), P())
    return jax.shard_map(shards, mesh=mesh, in_specs=in_specs, out_specs=out_specs, check_vma=False)
```

profile of v0, /device:TPU:1, one launch (start us, length us, event | category | flops | bytes accessed | tf_op | source)
XLA Modules:
  0.0 478.8 jit_solution(10044351522613762331)
XLA Ops:
  7.2 0.7 all-gather.2.cloned.1.call-update
  7.9 101.4 %all-gather.2.cloned.1.call-done = bf16[16384,512]{1,0:T(8,128)(2,1)} async-done(((bf16[1024,512]{1,0:T(8,128)(2,1)}), bf16[16384,512]{1,0:T(8,128)(2,1)}) %all-gather.2.cloned.1.call-update) | async-done | bytes 16777232 | tf_op jit(solution)/shard_map/all_gather | solution.py:10
  109.4 13.4 %fusion.34 = f32[256,512]{1,0:T(8,128)} fusion(bf16[256,16384]{1,0:T(8,128)(2,1)} %param.2, bf16[16384,512]{1,0:T(8,128)(2,1)} %all-gather.2.cloned.1.call-done), kind=kOutput, calls=%fused_computation.71 | convolution fusion | flops 4294967296 | bytes 25690112 | tf_op jit(solution)/shard_map/dot_general | solution.py:8
  123.1 91.7 %all-reduce.4.cloned.1.call-done = f32[256,512]{1,0:T(8,128)} async-done(((f32[256,512]{1,0:T(8,128)}), f32[256,512]{1,0:T(8,128)}) %all-reduce.4.cloned.1.call-update) | async-done | bytes 524304 | tf_op jit(solution)/shard_map/psum | solution.py:23
  214.8 3.2 fusion.35
  218.1 113.7 %all-reduce.6.cloned.1.call-done = f32[512,512]{0,1:T(8,128)} async-done(((f32[512,512]{0,1:T(8,128)}), f32[512,512]{0,1:T(8,128)}) %all-reduce.6.cloned.1.call-update) | async-done | bytes 1048592 | tf_op jit(solution)/shard_map/psum | solution.py:24
  331.8 1.3 broadcast_multiply_fusion
  333.5 1.5 fusion
  334.9 11.7 %cholesky.104 = f32[128,128]{1,0:T(8,128)S(1)} custom-call(f32[128,128]{1,0:T(8,128)S(1)} %cholesky.266), custom_call_target="Cholesky" | custom-call | tf_op jit(solution)/shard_map/jit(cholesky)/cholesky | solution.py:27
  346.7 9.8 %custom-call.30 = f32[1,128,128]{1,2,0:T(8,128)S(1)} custom-call(f32[1,128,128]{2,1,0:T(8,128)S(1)} %get-tuple-element.33), custom_call_target="InvertDiagBlocksLowerTriangular" | custom-call | tf_op jit(solution)/shard_map/jit(cholesky)/cholesky | solution.py:27
  357.3 11.8 %cholesky.217 = f32[128,128]{1,0:T(8,128)S(1)} custom-call(f32[128,128]{1,0:T(8,128)S(1)} %cholesky.270), custom_call_target="Cholesky" | custom-call | tf_op jit(solution)/shard_map/jit(cholesky)/cholesky | solution.py:27
  369.2 9.8 %custom-call.31 = f32[1,128,128]{1,2,0:T(8,128)S(1)} custom-call(f32[1,128,128]{2,1,0:T(8,128)S(1)} %get-tuple-element.30), custom_call_target="InvertDiagBlocksLowerTriangular" | custom-call | tf_op jit(solution)/shard_map/jit(cholesky)/cholesky | solution.py:27
  379.7 11.7 %cholesky.238 = f32[128,128]{1,0:T(8,128)S(1)} custom-call(f32[128,128]{1,0:T(8,128)S(1)} %cholesky.275), custom_call_target="Cholesky" | custom-call | tf_op jit(solution)/shard_map/jit(cholesky)/cholesky | solution.py:27
  391.4 0.7 compare_reduce_fusion.1
  392.1 9.8 %custom-call.32 = f32[1,128,128]{1,2,0:T(8,128)S(1)} custom-call(f32[1,128,128]{2,1,0:T(8,128)S(1)} %get-tuple-element.27), custom_call_target="InvertDiagBlocksLowerTriangular" | custom-call | tf_op jit(solution)/shard_map/jit(cholesky)/cholesky | solution.py:27
  402.6 12.0 %cholesky.255 = f32[128,128]{1,0:T(8,128)S(1)} custom-call(f32[128,128]{1,0:T(8,128)S(1)} %convolution_subtract_fusion.2), custom_call_target="Cholesky" | custom-call | tf_op jit(solution)/shard_map/jit(cholesky)/cholesky | solution.py:27
  414.6 0.6 compare_reduce_fusion
  415.2 0.7 compare_reduce_fusion.2
  418.7 1.3 copy.6
  420.0 8.1 %while.1 = (s32[]{:T(128)}, f32[512,512]{1,0:T(8,128)S(1)}, s32[4,2]{0,1:T(2,128)S(1)}, f32[4,128,128]{2,1,0:T(8,128)S(1)}, s32[]{:T(128)}) while((s32[]{:T(128)}, f32[512,512]{1,0:T(8,128)S(1)}, s32[4,2]{0,1:T(2,128)S(1)}, f32[4,128,128]{2,1,0:T(8,128)S(1)}, s32[]{:T(128)}) %tuple.33), condition=%wide.while_cond, body=%wide.while_body.sunk | while | flops 2 | bytes 131181 | solution.py:28
  420.6 1.3 bitcast_dynamic-update-slice_fusion.2
  422.1 0.6 fusion.46
  422.7 1.3 bitcast_dynamic-update-slice_fusion.2
  424.7 1.3 bitcast_dynamic-update-slice_fusion.2
  426.2 0.6 fusion.46
  426.8 1.3 bitcast_dynamic-update-slice_fusion.2
  428.1 39.3 %custom-call.33 = f32[4,128,128]{1,2,0:T(8,128)S(1)} custom-call(f32[4,128,128]{2,1,0:T(8,128)S(1)} %get-tuple-element.9), custom_call_target="InvertDiagBlocksLowerTriangular" | custom-call | tf_op jit(solution)/shard_map/triangular_solve | solution.py:28
  467.4 0.9 fusion.15
  468.3 0.9 convolution_subtract_fusion.5
  469.4 0.9 convolution_subtract_fusion.4
  470.5 1.0 convolution_subtract_fusion.3
  471.7 0.6 pad_maximum_fusion
  (33 shorter events, 5.1 us)
Async XLA Ops:
  7.2 102.2 %all-gather.2.cloned.1.call-start = ((), (), s32[]{:S(2)}) async-start(), calls=%async_computation | async-start | bytes 17825792 | tf_op jit(solution)/shard_map/all_gather | solution.py:10
  7.9 206.9 %all-reduce.4.cloned.1.call-start = ((), (), s32[]{:S(2)}) async-start(), calls=%async_computation.1 | async-start | bytes 1048576 | tf_op jit(solution)/shard_map/psum | solution.py:23
  122.8 209.0 %all-reduce.6.cloned.1.call-start = ((), (), s32[]{:S(2)}) async-start(), calls=%async_computation.2 | async-start | bytes 2097152 | tf_op jit(solution)/shard_map/psum | solution.py:24
Sparse Core Ops, SparseCore 0:
  9.8 99.5 all-gather.1
  123.0 91.8 all-reduce.3
  218.2 113.5 all-reduce.5
where the time goes:
time: 479 us
  waiting for transfers between devices  308 us (64%)
  other arithmetic  122 us (25%)
  matrix products  22.7 us (5%)
  between operations  16.5 us (3%)
  local copies, waits for them, and re-layouts  9.84 us (2%)
    psum x1, waiting for transfers between devices, shards(): gram = lax.psum(gram_term(sketch), 'row')  114 us
    all_gather x1, waiting for transfers between devices, probe_product(): lax.all_gather(test_matrix, 'row', axis=0, tiled=True)  101 us
    psum x1, waiting for transfers between devices, shards(): sketch = lax.psum(partial_value, 'col')  91.7 us
    another operation x14, other arithmetic, shards(): lower_factor = jnp.linalg.cholesky(gram)  78.8 us
    another operation x3, other arithmetic, shards(): lax.linalg.triangular_solve(lower_factor, own_rows, left_side=False, lowe...  40 us
    dot_general x1, matrix products, probe_product(): jnp.dot(matrix, lax.all_gather(test_matrix, 'row', axis=0, tiled=True), p...  13.4 us
  transfers between devices with their start and end apart: 3, of which 3 were waited for; matrix products, arithmetic and copies ran while one was open for 0% of the time, Pallas kernels for 0%

commit v1 on v0

--- a/solution.py
+++ b/solution.py
@@ -4,12 +4,24 @@
 from jax.sharding import PartitionSpec as P
 
 
+def collect(x, axis, dim):
+    ways, here, hop = (lax.axis_size(axis), lax.axis_index(axis), x.shape[dim])
+    shape = [n * ways if d == dim else n for d, n in enumerate(x.shape)]
+    full = lax.dynamic_update_slice_in_dim(jnp.zeros(shape, x.dtype), x, here * hop, axis=dim)
+    going_up = going_down = x
+    for far in range(1, ways // 2 + 1):
+        going_up = lax.ppermute(going_up, axis, [(d, (d + 1) % ways) for d in range(ways)])
+        full = lax.dynamic_update_slice_in_dim(full, going_up, (here - far) % ways * hop, axis=dim)
+        if 2 * far < ways:
+            going_down = lax.ppermute(going_down, axis, [(d, (d - 1) % ways) for d in range(ways)])
+            full = lax.dynamic_update_slice_in_dim(
+                full, going_down, (here + far) % ways * hop, axis=dim
+            )
+    return full
+
+
 def probe_product(matrix, test_matrix):
-    return jnp.dot(
-        matrix,
-        lax.all_gather(test_matrix, "row", axis=0, tiled=True),
-        preferred_element_type=jnp.float32,
-    )
+    return jnp.dot(matrix, collect(test_matrix, "row", 0), preferred_element_type=jnp.float32)
 
 
 def gram_term(own_rows):

time: 479 us -> 512 us (1.069)
  starting transfers between devices: 0.3 us -> 46.4 us
  waiting for transfers between devices: 308 us -> 263 us
  local copies, waits for them, and re-layouts: 9.84 us -> 43.6 us
    all_gather x1 -> x0, waiting for transfers between devices: 101 us -> none  [probe_product(): lax.all_gather(test_matrix, 'row', axis=0, tiled=True)]
    ppermute x0 -> x15, waiting for transfers between devices: none -> 50.6 us  [the longest x8 48.1 us: collect(): lax.ppermute(going_up, axis, [(d, (d + 1) % ways) for d in range(ways)])]
    ppermute x0 -> x15, starting transfers between devices: none -> 46.2 us  [the longest x7 28.3 us: collect(): lax.ppermute(going_down, axis, [(d, (d - 1) % ways) for d in range(ways)])]
    dynamic_update_slice x0 -> x16, local copies, waits for them, and re-layouts: none -> 22 us  [the longest x8 11 us: collect(): lax.dynamic_update_slice_in_dim(full, going_up, (here - far) % ways * hop...]
    broadcast_in_dim x0 -> x1, local copies, waits for them, and re-layouts: none -> 7.74 us  [collect(): jnp.zeros(shape, x.dtype)]
    psum x1, waiting for transfers between devices: 91.7 us -> 98.9 us  [shards(): sketch = lax.psum(partial_value, 'col')]
  transfers between devices with their start and end apart: 3 -> 17, of which waited for: 3 -> 13; matrix products, arithmetic and copies ran while one was open for 0% -> 6% of each run, Pallas kernels for 0% -> 0%
where the time goes in v1:
time: 512 us
  waiting for transfers between devices  263 us (51%)
  other arithmetic  123 us (24%)
  starting transfers between devices  46.4 us (9%)
  local copies, waits for them, and re-layouts  43.6 us (9%)
  matrix products  19 us (4%)
  between operations  16.8 us (3%)
    psum x1, waiting for transfers between devices, shards(): gram = lax.psum(gram_term(sketch), 'row')  114 us
    psum x1, waiting for transfers between devices, shards(): sketch = lax.psum(partial_value, 'col')  98.9 us
    another operation x14, other arithmetic, shards(): lower_factor = jnp.linalg.cholesky(gram)  78.8 us
    ppermute x8, waiting for transfers between devices, collect(): lax.ppermute(going_up, axis, [(d, (d + 1) % ways) for d in range(ways)])  48.1 us
    another operation x3, other arithmetic, shards(): lax.linalg.triangular_solve(lower_factor, own_rows, left_side=False, lowe...  40 us
    ppermute x7, starting transfers between devices, collect(): lax.ppermute(going_down, axis, [(d, (d - 1) % ways) for d in range(ways)])  28.3 us
    ppermute x8, starting transfers between devices, collect(): lax.ppermute(going_up, axis, [(d, (d + 1) % ways) for d in range(ways)])  17.9 us
    another operation x12, local copies, waits for them, and re-layouts  11.1 us
  transfers between devices with their start and end apart: 17, of which 13 were waited for; matrix products, arithmetic and copies ran while one was open for 6% of the time, Pallas kernels for 0%

profile of v1, /device:TPU:1, one launch (start us, length us, event | category | flops | bytes accessed | tf_op | source)
XLA Modules:
  0.0 511.8 jit_solution(2066119512491011913)
XLA Ops:
  7.2 3.0 collective-permute-start
  10.5 11.8 %collective-permute-done = bf16[1024,512]{1,0:T(8,128)(2,1)S(1)} collective-permute-done((bf16[1024,512]{1,0:T(8,128)(2,1)}, bf16[1024,512]{1,0:T(8,128)(2,1)S(1)}, u32[]{:S(2)}, u32[]{:S(2)}) %collective-permute-start) | collective-permute-done | bytes 1048608 | tf_op jit(solution)/shard_map/ppermute | solution.py:13
  22.3 2.4 collective-permute-start.2
  26.7 9.7 %collective-permute-done.2 = bf16[1024,512]{1,0:T(8,128)(2,1)S(1)} collective-permute-done((bf16[1024,512]{1,0:T(8,128)(2,1)S(1)}, bf16[1024,512]{1,0:T(8,128)(2,1)S(1)}, u32[]{:S(2)}, u32[]{:S(2)}) %collective-permute-start.2) | collective-permute-done | bytes 1048608 | tf_op jit(solution)/shard_map/ppermute | solution.py:13
  36.4 2.5 collective-permute-start.4
  39.5 2.7 collective-permute-start.5
  42.2 8.5 %collective-permute-done.4 = bf16[1024,512]{1,0:T(8,128)(2,1)S(1)} collective-permute-done((bf16[1024,512]{1,0:T(8,128)(2,1)S(1)}, bf16[1024,512]{1,0:T(8,128)(2,1)S(1)}, u32[]{:S(2)}, u32[]{:S(2)}) %collective-permute-start.4) | collective-permute-done | bytes 1048608 | tf_op jit(solution)/shard_map/ppermute | solution.py:13
  50.7 2.5 collective-permute-start.6
  54.0 3.6 collective-permute-start.7
  57.6 7.2 %collective-permute-done.6 = bf16[1024,512]{1,0:T(8,128)(2,1)S(1)} collective-permute-done((bf16[1024,512]{1,0:T(8,128)(2,1)S(1)}, bf16[1024,512]{1,0:T(8,128)(2,1)S(1)}, u32[]{:S(2)}, u32[]{:S(2)}) %collective-permute-start.6) | collective-permute-done | bytes 1048608 | tf_op jit(solution)/shard_map/ppermute | solution.py:13
  65.9 2.5 collective-permute-start.8
  68.5 5.5 %collective-permute-start.9 = (bf16[1024,512]{1,0:T(8,128)(2,1)S(1)}, bf16[1024,512]{1,0:T(8,128)(2,1)}, u32[]{:S(2)}, u32[]{:S(2)}) collective-permute-start(bf16[1024,512]{1,0:T(8,128)(2,1)S(1)} %collective-permute-done.7), channel_id=1, source_target_pairs={{0,240},{16,0},{32,16},{48,32},{64,48},{80,64},{96,80},{112,96},{1... | collective-permute-start | bytes 3145736 | tf_op jit(solution)/shard_map/ppermute | solution.py:16
  74.0 6.1 %collective-permute-done.8 = bf16[1024,512]{1,0:T(8,128)(2,1)S(1)} collective-permute-done((bf16[1024,512]{1,0:T(8,128)(2,1)S(1)}, bf16[1024,512]{1,0:T(8,128)(2,1)S(1)}, u32[]{:S(2)}, u32[]{:S(2)}) %collective-permute-start.8) | collective-permute-done | bytes 1048608 | tf_op jit(solution)/shard_map/ppermute | solution.py:13
  80.1 2.5 collective-permute-start.10
  83.1 6.4 %collective-permute-start.11 = (bf16[1024,512]{1,0:T(8,128)(2,1)}, bf16[1024,512]{1,0:T(8,128)(2,1)}, u32[]{:S(2)}, u32[]{:S(2)}) collective-permute-start(bf16[1024,512]{1,0:T(8,128)(2,1)} %collective-permute-done.9), channel_id=1, source_target_pairs={{0,240},{16,0},{32,16},{48,32},{64,48},{80,64},{96,80},{112,96},{1... | collective-permute-start | bytes 3145736 | tf_op jit(solution)/shard_map/ppermute | solution.py:16
  89.5 4.8 collective-permute-done.10
  94.3 2.6 collective-permute-start.12
  96.9 7.7 %broadcast_in_dim.5 = bf16[16384,512]{1,0:T(8,128)(2,1)} broadcast(bf16[]{:T(256)} %constant.229.clone.1), dimensions={} | broadcast | bytes 16777218 | tf_op jit(solution)/shard_map/broadcast_in_dim | solution.py:10
  111.0 8.1 %collective-permute-start.13 = (bf16[1024,512]{1,0:T(8,128)(2,1)}, bf16[1024,512]{1,0:T(8,128)(2,1)S(1)}, u32[]{:S(2)}, u32[]{:S(2)}) collective-permute-start(bf16[1024,512]{1,0:T(8,128)(2,1)} %collective-permute-done.11), channel_id=1, source_target_pairs={{0,240},{16,0},{32,16},{48,32},{64,48},{80,64},{96,80},{112,96},{1... | collective-permute-start | bytes 3145736 | tf_op jit(solution)/shard_map/ppermute | solution.py:16
  134.8 9.1 %convolution_bitcast_fusion = f32[256,512]{0,1:T(8,128)} fusion(bf16[16384,512]{1,0:T(8,128)(2,1)} %constant_dynamic-update-slice_fusion.1, bf16[256,16384]{1,0:T(8,128)(2,1)S(1)} %bitcast.54), kind=kOutput, calls=%fused_computation.2 | convolution fusion | flops 4294967296 | bytes 25690112 | tf_op jit(solution)/shard_map/dot_general | solution.py:24
  144.2 98.9 %all-reduce.4.cloned.1.call-done = f32[256,512]{0,1:T(8,128)} async-done(((f32[256,512]{0,1:T(8,128)}), f32[256,512]{0,1:T(8,128)}) %all-reduce.4.cloned.1.call-update) | async-done | bytes 524304 | tf_op jit(solution)/shard_map/psum | solution.py:35
  243.1 3.3 fusion.37
  246.4 113.7 %all-reduce.6.cloned.1.call-done = f32[512,512]{0,1:T(8,128)} async-done(((f32[512,512]{0,1:T(8,128)}), f32[512,512]{0,1:T(8,128)}) %all-reduce.6.cloned.1.call-update) | async-done | bytes 1048592 | tf_op jit(solution)/shard_map/psum | solution.py:36
  363.3 11.7 %cholesky.104 = f32[128,128]{1,0:T(8,128)S(1)} custom-call(f32[128,128]{1,0:T(8,128)S(1)} %cholesky.266), custom_call_target="Cholesky" | custom-call | tf_op jit(solution)/shard_map/jit(cholesky)/cholesky | solution.py:39
  375.1 9.8 %custom-call.30 = f32[1,128,128]{1,2,0:T(8,128)S(1)} custom-call(f32[1,128,128]{2,1,0:T(8,128)S(1)} %get-tuple-element.33), custom_call_target="InvertDiagBlocksLowerTriangular" | custom-call | tf_op jit(solution)/shard_map/jit(cholesky)/cholesky | solution.py:39
  385.6 11.8 %cholesky.217 = f32[128,128]{1,0:T(8,128)S(1)} custom-call(f32[128,128]{1,0:T(8,128)S(1)} %cholesky.270), custom_call_target="Cholesky" | custom-call | tf_op jit(solution)/shard_map/jit(cholesky)/cholesky | solution.py:39
  397.5 9.8 %custom-call.31 = f32[1,128,128]{1,2,0:T(8,128)S(1)} custom-call(f32[1,128,128]{2,1,0:T(8,128)S(1)} %get-tuple-element.30), custom_call_target="InvertDiagBlocksLowerTriangular" | custom-call | tf_op jit(solution)/shard_map/jit(cholesky)/cholesky | solution.py:39
  408.0 11.7 %cholesky.238 = f32[128,128]{1,0:T(8,128)S(1)} custom-call(f32[128,128]{1,0:T(8,128)S(1)} %cholesky.275), custom_call_target="Cholesky" | custom-call | tf_op jit(solution)/shard_map/jit(cholesky)/cholesky | solution.py:39
  420.4 9.8 %custom-call.32 = f32[1,128,128]{1,2,0:T(8,128)S(1)} custom-call(f32[1,128,128]{2,1,0:T(8,128)S(1)} %get-tuple-element.27), custom_call_target="InvertDiagBlocksLowerTriangular" | custom-call | tf_op jit(solution)/shard_map/jit(cholesky)/cholesky | solution.py:39
  430.8 12.0 %cholesky.255 = f32[128,128]{1,0:T(8,128)S(1)} custom-call(f32[128,128]{1,0:T(8,128)S(1)} %convolution_subtract_fusion.2), custom_call_target="Cholesky" | custom-call | tf_op jit(solution)/shard_map/jit(cholesky)/cholesky | solution.py:39
  447.8 11.1 %while.1 = (s32[]{:T(128)}, f32[512,512]{1,0:T(8,128)}, s32[4,2]{0,1:T(2,128)S(1)}, f32[4,128,128]{2,1,0:T(8,128)S(1)}, s32[]{:T(128)}) while((s32[]{:T(128)}, f32[512,512]{1,0:T(8,128)}, s32[4,2]{0,1:T(2,128)S(1)}, f32[4,128,128]{2,1,0:T(8,128)S(1)}, s32[]{:T(128)}) %tuple.33), condition=%wide.while_cond, body=%wide.while_body.sunk | while | flops 2 | bytes 131181 | solution.py:40
  459.0 39.3 %custom-call.33 = f32[4,128,128]{1,2,0:T(8,128)S(1)} custom-call(f32[4,128,128]{2,1,0:T(8,128)S(1)} %get-tuple-element.9), custom_call_target="InvertDiagBlocksLowerTriangular" | custom-call | tf_op jit(solution)/shard_map/triangular_solve | solution.py:40
  (114 shorter events, 53.9 us)
Async XLA Ops:
  7.2 97.5 %copy-start.1 = (bf16[1024,512]{1,0:T(8,128)(2,1)S(1)}, bf16[1024,512]{1,0:T(8,128)(2,1)}, u32[]{:S(2)}) copy-start(bf16[1024,512]{1,0:T(8,128)(2,1)} %param.3) | copy-start | bytes 3145732
  7.2 235.9 %all-reduce.4.cloned.1.call-start = ((), (), s32[]{:S(2)}) async-start(), calls=%async_computation | async-start | bytes 1048576 | tf_op jit(solution)/shard_map/psum | solution.py:35
  7.2 15.1 %collective-permute-start = (bf16[1024,512]{1,0:T(8,128)(2,1)}, bf16[1024,512]{1,0:T(8,128)(2,1)S(1)}, u32[]{:S(2)}, u32[]{:S(2)}) collective-permute-start(bf16[1024,512]{1,0:T(8,128)(2,1)} %param.3), channel_id=1, source_target_pairs={{0,16},{16,32},{32,48},{48,64},{64,80},{80,96},{96,112},{112,128},... | collective-permute-start | bytes 3145736 | tf_op jit(solution)/shard_map/ppermute | solution.py:13
  10.2 14.7 %collective-permute-start.1 = (bf16[1024,512]{1,0:T(8,128)(2,1)}, bf16[1024,512]{1,0:T(8,128)(2,1)S(1)}, u32[]{:S(2)}, u32[]{:S(2)}) collective-permute-start(bf16[1024,512]{1,0:T(8,128)(2,1)} %param.3), channel_id=1, source_target_pairs={{0,240},{16,0},{32,16},{48,32},{64,48},{80,64},{96,80},{112,96},{1... | collective-permute-start | bytes 3145736 | tf_op jit(solution)/shard_map/ppermute | solution.py:16
  22.3 14.1 %collective-permute-start.2 = (bf16[1024,512]{1,0:T(8,128)(2,1)S(1)}, bf16[1024,512]{1,0:T(8,128)(2,1)S(1)}, u32[]{:S(2)}, u32[]{:S(2)}) collective-permute-start(bf16[1024,512]{1,0:T(8,128)(2,1)S(1)} %collective-permute-done), channel_id=1, source_target_pairs={{0,16},{16,32},{32,48},{48,64},{64,80},{80,96},{96,112},{112,128},... | collective-permute-start | bytes 3145736 | tf_op jit(solution)/shard_map/ppermute | solution.py:13
  25.0 14.5 %collective-permute-start.3 = (bf16[1024,512]{1,0:T(8,128)(2,1)S(1)}, bf16[1024,512]{1,0:T(8,128)(2,1)S(1)}, u32[]{:S(2)}, u32[]{:S(2)}) collective-permute-start(bf16[1024,512]{1,0:T(8,128)(2,1)S(1)} %collective-permute-done.1), channel_id=1, source_target_pairs={{0,240},{16,0},{32,16},{48,32},{64,48},{80,64},{96,80},{112,96},{1... | collective-permute-start | bytes 3145736 | tf_op jit(solution)/shard_map/ppermute | solution.py:16
  36.4 14.2 %collective-permute-start.4 = (bf16[1024,512]{1,0:T(8,128)(2,1)S(1)}, bf16[1024,512]{1,0:T(8,128)(2,1)S(1)}, u32[]{:S(2)}, u32[]{:S(2)}) collective-permute-start(bf16[1024,512]{1,0:T(8,128)(2,1)S(1)} %collective-permute-done.2), channel_id=1, source_target_pairs={{0,16},{16,32},{32,48},{48,64},{64,80},{80,96},{96,112},{112,128},... | collective-permute-start | bytes 3145736 | tf_op jit(solution)/shard_map/ppermute | solution.py:13
  39.5 13.6 %copy-start.10 = (bf16[1024,512]{1,0:T(8,128)(2,1)}, bf16[1024,512]{1,0:T(8,128)(2,1)S(1)}, u32[]{:S(2)}) copy-start(bf16[1024,512]{1,0:T(8,128)(2,1)S(1)} %collective-permute-done.3) | copy-start | bytes 3145732
  39.5 14.5 %collective-permute-start.5 = (bf16[1024,512]{1,0:T(8,128)(2,1)S(1)}, bf16[1024,512]{1,0:T(8,128)(2,1)S(1)}, u32[]{:S(2)}, u32[]{:S(2)}) collective-permute-start(bf16[1024,512]{1,0:T(8,128)(2,1)S(1)} %collective-permute-done.3), channel_id=1, source_target_pairs={{0,240},{16,0},{32,16},{48,32},{64,48},{80,64},{96,80},{112,96},{1... | collective-permute-start | bytes 3145736 | tf_op jit(solution)/shard_map/ppermute | solution.py:16
  50.7 14.2 %collective-permute-start.6 = (bf16[1024,512]{1,0:T(8,128)(2,1)S(1)}, bf16[1024,512]{1,0:T(8,128)(2,1)S(1)}, u32[]{:S(2)}, u32[]{:S(2)}) collective-permute-start(bf16[1024,512]{1,0:T(8,128)(2,1)S(1)} %collective-permute-done.4), channel_id=1, source_target_pairs={{0,16},{16,32},{32,48},{48,64},{64,80},{80,96},{96,112},{112,128},... | collective-permute-start | bytes 3145736 | tf_op jit(solution)/shard_map/ppermute | solution.py:13
  54.0 29.0 %copy-start.8 = (bf16[1024,512]{1,0:T(8,128)(2,1)}, bf16[1024,512]{1,0:T(8,128)(2,1)S(1)}, u32[]{:S(2)}) copy-start(bf16[1024,512]{1,0:T(8,128)(2,1)S(1)} %collective-permute-done.5) | copy-start | bytes 3145732
  54.0 14.5 %collective-permute-start.7 = (bf16[1024,512]{1,0:T(8,128)(2,1)S(1)}, bf16[1024,512]{1,0:T(8,128)(2,1)S(1)}, u32[]{:S(2)}, u32[]{:S(2)}) collective-permute-start(bf16[1024,512]{1,0:T(8,128)(2,1)S(1)} %collective-permute-done.5), channel_id=1, source_target_pairs={{0,240},{16,0},{32,16},{48,32},{64,48},{80,64},{96,80},{112,96},{1... | collective-permute-start | bytes 3145736 | tf_op jit(solution)/shard_map/ppermute | solution.py:16
  65.9 14.2 %collective-permute-start.8 = (bf16[1024,512]{1,0:T(8,128)(2,1)S(1)}, bf16[1024,512]{1,0:T(8,128)(2,1)S(1)}, u32[]{:S(2)}, u32[]{:S(2)}) collective-permute-start(bf16[1024,512]{1,0:T(8,128)(2,1)S(1)} %collective-permute-done.6), channel_id=1, source_target_pairs={{0,16},{16,32},{32,48},{48,64},{64,80},{80,96},{96,112},{112,128},... | collective-permute-start | bytes 3145736 | tf_op jit(solution)/shard_map/ppermute | solution.py:13
  68.5 11.5 %copy-start.6 = (bf16[1024,512]{1,0:T(8,128)(2,1)}, bf16[1024,512]{1,0:T(8,128)(2,1)S(1)}, u32[]{:S(2)}) copy-start(bf16[1024,512]{1,0:T(8,128)(2,1)S(1)} %collective-permute-done.7) | copy-start | bytes 3145732
  68.5 14.5 %collective-permute-start.9 = (bf16[1024,512]{1,0:T(8,128)(2,1)S(1)}, bf16[1024,512]{1,0:T(8,128)(2,1)}, u32[]{:S(2)}, u32[]{:S(2)}) collective-permute-start(bf16[1024,512]{1,0:T(8,128)(2,1)S(1)} %collective-permute-done.7), channel_id=1, source_target_pairs={{0,240},{16,0},{32,16},{48,32},{64,48},{80,64},{96,80},{112,96},{1... | collective-permute-start | bytes 3145736 | tf_op jit(solution)/shard_map/ppermute | solution.py:16
  80.1 9.4 %copy-start.12 = (bf16[1024,512]{1,0:T(8,128)(2,1)}, bf16[1024,512]{1,0:T(8,128)(2,1)S(1)}, u32[]{:S(2)}) copy-start(bf16[1024,512]{1,0:T(8,128)(2,1)S(1)} %collective-permute-done.8) | copy-start | bytes 3145732
  80.1 14.2 %collective-permute-start.10 = (bf16[1024,512]{1,0:T(8,128)(2,1)S(1)}, bf16[1024,512]{1,0:T(8,128)(2,1)}, u32[]{:S(2)}, u32[]{:S(2)}) collective-permute-start(bf16[1024,512]{1,0:T(8,128)(2,1)S(1)} %collective-permute-done.8), channel_id=1, source_target_pairs={{0,16},{16,32},{32,48},{48,64},{64,80},{80,96},{96,112},{112,128},... | collective-permute-start | bytes 3145736 | tf_op jit(solution)/shard_map/ppermute | solution.py:13
  83.1 28.0 %collective-permute-start.11 = (bf16[1024,512]{1,0:T(8,128)(2,1)}, bf16[1024,512]{1,0:T(8,128)(2,1)}, u32[]{:S(2)}, u32[]{:S(2)}) collective-permute-start(bf16[1024,512]{1,0:T(8,128)(2,1)} %collective-permute-done.9), channel_id=1, source_target_pairs={{0,240},{16,0},{32,16},{48,32},{64,48},{80,64},{96,80},{112,96},{1... | collective-permute-start | bytes 3145736 | tf_op jit(solution)/shard_map/ppermute | solution.py:16
  94.3 25.9 %collective-permute-start.12 = (bf16[1024,512]{1,0:T(8,128)(2,1)}, bf16[1024,512]{1,0:T(8,128)(2,1)}, u32[]{:S(2)}, u32[]{:S(2)}) collective-permute-start(bf16[1024,512]{1,0:T(8,128)(2,1)} %collective-permute-done.10), channel_id=1, source_target_pairs={{0,16},{16,32},{32,48},{48,64},{64,80},{80,96},{96,112},{112,128},... | collective-permute-start | bytes 3145736 | tf_op jit(solution)/shard_map/ppermute | solution.py:13
  96.9 10.9 %copy-start.5 = (bf16[1024,512]{1,0:T(8,128)(2,1)S(1)}, bf16[1024,512]{1,0:T(8,128)(2,1)}, u32[]{:S(2)}) copy-start(bf16[1024,512]{1,0:T(8,128)(2,1)} %copy-done.4) | copy-start | bytes 3145732
  96.9 12.0 %copy-start.11 = (bf16[1024,512]{1,0:T(8,128)(2,1)S(1)}, bf16[1024,512]{1,0:T(8,128)(2,1)}, u32[]{:S(2)}) copy-start(bf16[1024,512]{1,0:T(8,128)(2,1)} %copy-done.10) | copy-start | bytes 3145732
  96.9 13.0 %copy-start.15 = (bf16[1024,512]{1,0:T(8,128)(2,1)S(1)}, bf16[1024,512]{1,0:T(8,128)(2,1)}, u32[]{:S(2)}) copy-start(bf16[1024,512]{1,0:T(8,128)(2,1)} %copy-done.14) | copy-start | bytes 3145732
  96.9 22.2 %copy-start.9 = (bf16[1024,512]{1,0:T(8,128)(2,1)S(1)}, bf16[1024,512]{1,0:T(8,128)(2,1)}, u32[]{:S(2)}) copy-start(bf16[1024,512]{1,0:T(8,128)(2,1)} %copy-done.8) | copy-start | bytes 3145732
  96.9 23.3 %copy-start.3 = (bf16[1024,512]{1,0:T(8,128)(2,1)S(1)}, bf16[1024,512]{1,0:T(8,128)(2,1)}, u32[]{:S(2)}) copy-start(bf16[1024,512]{1,0:T(8,128)(2,1)} %copy-done.2) | copy-start | bytes 3145732
  96.9 24.3 %copy-start.7 = (bf16[1024,512]{1,0:T(8,128)(2,1)S(1)}, bf16[1024,512]{1,0:T(8,128)(2,1)}, u32[]{:S(2)}) copy-start(bf16[1024,512]{1,0:T(8,128)(2,1)} %copy-done.6) | copy-start | bytes 3145732
  96.9 25.4 %copy-start.13 = (bf16[1024,512]{1,0:T(8,128)(2,1)S(1)}, bf16[1024,512]{1,0:T(8,128)(2,1)}, u32[]{:S(2)}) copy-start(bf16[1024,512]{1,0:T(8,128)(2,1)} %copy-done.12) | copy-start | bytes 3145732
  104.7 30.1 %slice-start = ((s8[8388608]{0:T(1024)(128)(4,1)}), s8[4194304]{0:T(1024)(128)(4,1)S(1)}, s32[]{:S(2)}) async-start(s8[8388608]{0:T(1024)(128)(4,1)} %bitcast.53), calls=%async_computation.2 | async-start | bytes 8388608
  111.0 21.6 %collective-permute-start.13 = (bf16[1024,512]{1,0:T(8,128)(2,1)}, bf16[1024,512]{1,0:T(8,128)(2,1)S(1)}, u32[]{:S(2)}, u32[]{:S(2)}) collective-permute-start(bf16[1024,512]{1,0:T(8,128)(2,1)} %collective-permute-done.11), channel_id=1, source_target_pairs={{0,240},{16,0},{32,16},{48,32},{64,48},{80,64},{96,80},{112,96},{1... | collective-permute-start | bytes 3145736 | tf_op jit(solution)/shard_map/ppermute | solution.py:16
  120.2 13.6 %collective-permute-start.14 = (bf16[1024,512]{1,0:T(8,128)(2,1)}, bf16[1024,512]{1,0:T(8,128)(2,1)S(1)}, u32[]{:S(2)}, u32[]{:S(2)}) collective-permute-start(bf16[1024,512]{1,0:T(8,128)(2,1)} %collective-permute-done.12), channel_id=1, source_target_pairs={{0,16},{16,32},{32,48},{48,64},{64,80},{80,96},{96,112},{112,128},... | collective-permute-start | bytes 3145736 | tf_op jit(solution)/shard_map/ppermute | solution.py:13
  121.2 13.6 %slice-start.1 = ((s8[8388608]{0:T(1024)(128)(4,1)}), s8[4194304]{0:T(1024)(128)(4,1)S(1)}, s32[]{:S(2)}) async-start(s8[8388608]{0:T(1024)(128)(4,1)} %bitcast.53), calls=%async_computation.3 | async-start | bytes 8388608
  144.0 216.2 %all-reduce.6.cloned.1.call-start = ((), (), s32[]{:S(2)}) async-start(), calls=%async_computation.1 | async-start | bytes 2097152 | tf_op jit(solution)/shard_map/psum | solution.py:36
  243.1 255.2 %copy-start = (f32[256,512]{0,1:T(8,128)S(1)}, f32[256,512]{0,1:T(8,128)}, u32[]{:S(2)}) copy-start(f32[256,512]{0,1:T(8,128)} %all-reduce.4.cloned.1.call-done) | copy-start | bytes 1572868
  (3 other events, 13.7 us)
Sparse Core Ops, SparseCore 0:
  144.1 98.9 all-reduce.3
  246.5 113.5 all-reduce.5
